TPU v7x, 32 devices: a whole 2x2x4 slice. The times are simulated.
32 devices in a mesh: job: 2 (over x), space: 4 (over y, core), arc: 4 (over z).
Axes of the slice: x: 2, y: 2, z: 4, core: 2. Of those that a mesh axis runs over, the one named last changes fastest.
Arguments:
- saved_velocity_trajectory: bfloat16 [64, 3, 8, 128, 128], P(('job', 'arc'), None, 'space'), parts along dimension 0, may hold values from -4 to 4
- saved_warmth_trajectory: bfloat16 [64, 8, 128, 128], P(('job', 'arc'), 'space'), parts along dimension 0, may hold values from -5 to 5
- control_porosity: float32 [16, 128, 128], P(('job', 'space')), parts along dimension 0, may hold values from 0.05 to 1
- control_volume_flag: int32 [16, 128, 128], P(('job', 'space')), parts along dimension 0, may hold values 0 or 1
- entrance_face_flag: int32 [256, 128], P('job'), parts along dimension 0, may hold values 0 or 1
Outputs:
- gradient: float32 [16, 128, 128], P(('job', 'space'), 'arc'), parts along dimension 0
- entry_adjoint: float32 [8, 4, 8, 128, 128], P(('job', 'arc'), None, 'space'), parts along dimension 0
There are 2 independent parts, one for each index of `job`. A program takes and returns all parts, laid end to end along the dimension named above; each array names one. Nothing has to cross between parts.
All inputs are finite; a program needn't handle non-finite values. No bound on the sum of `control_volume_flag` on one device may be relied on, other than what follows from the above.
Results may differ from a plain program's by a relative error of at most 0.0003.
Values may be sent and summed in bfloat16 or wider, within the bound.
No kernel may reach another device: no remote copies, remote signals or barrier semaphores. Data moves between devices by JAX's collectives and lax.ppermute only.
A program may use at most 64 MiB of HBM per device.

v0:
```python
import jax
import jax.numpy as jnp
from jax import lax
from jax.sharding import PartitionSpec as P


def padded(cells, sides, width):
    for axis, dim in sides:
        count = lax.axis_size(axis)
        ends = count - 1
        head = lax.slice_in_dim(cells, 0, width, axis=dim)
        tail = lax.slice_in_dim(cells, cells.shape[dim] - width, cells.shape[dim], axis=dim)
        cells = jnp.concatenate(
            [
                lax.ppermute(tail, axis, [(i, (i + 1) % count) for i in range(ends)]),
                cells,
                lax.ppermute(head, axis, [((i + 1) % count, i) for i in range(ends)]),
            ],
            axis=dim,
        )
    return cells


def passed_along(value, axis, steps):
    count = lax.axis_size(axis)
    pairs = [(source, (source + steps) % count) for source in range(count)]
    return lax.ppermute(value, axis, pairs)


def laplace(ext):
    mid = ext[..., 1:-1, 1:-1, 1:-1]
    total = ext[..., 2:, 1:-1, 1:-1] + ext[..., :-2, 1:-1, 1:-1]
    total = total + ext[..., 1:-1, 2:, 1:-1] + ext[..., 1:-1, :-2, 1:-1]
    total = total + ext[..., 1:-1, 1:-1, 2:] + ext[..., 1:-1, 1:-1, :-2]
    return total - 6.0 * mid


def slopes(ext):
    return (
        0.5 * (ext[..., 2:, 1:-1, 1:-1] - ext[..., :-2, 1:-1, 1:-1]),
        0.5 * (ext[..., 1:-1, 2:, 1:-1] - ext[..., 1:-1, :-2, 1:-1]),
        0.5 * (ext[..., 1:-1, 1:-1, 2:] - ext[..., 1:-1, 1:-1, :-2]),
    )


def pad_sides(field, operating_variant):
    widths = [(0, 0)] * (field.ndim - 2) + [(1, 1), (1, 1)]
    return jnp.pad(field, widths, mode=operating_variant)


def adjoint_update(
    adj,
    ext_a,
    ext_b,
    padded_thermal_field,
    speed,
    alpha,
    porosity_sensitivity,
    solid,
    quadrature_factor,
):
    a_now = adj[:3]
    current_adjoint_vector = adj[3]
    grad_b = slopes(ext_b)
    grad_a = slopes(ext_a)
    grad_t = slopes(padded_thermal_field)
    carry_b = speed[0] * grad_b[0] + speed[1] * grad_b[1] + speed[2] * grad_b[2]
    carry_a = speed[0:1] * grad_a[0] + speed[1:2] * grad_a[1] + speed[2:3] * grad_a[2]
    thermal_current_field = padded_thermal_field[1:-1, 1:-1, 1:-1]
    grad_stack = jnp.stack(grad_t)
    new_a = a_now + 0.1 * (
        1.2 * laplace(ext_a) + carry_a - alpha * a_now - current_adjoint_vector * grad_stack
    )
    new_b = current_adjoint_vector + 0.1 * (
        1.2 * laplace(ext_b) + carry_b - 2.0 * solid * current_adjoint_vector + 2.0 * solid
    )
    common_divisor_lcm_like = jnp.sum(a_now * speed, axis=0)
    summand_contribution = (
        0.1
        * quadrature_factor
        * (
            porosity_sensitivity * common_divisor_lcm_like
            + 2.0 * (current_adjoint_vector - 1.0) * thermal_current_field
        )
    )
    return (jnp.concatenate([new_a, new_b[None]], axis=0), summand_contribution)


def body(
    saved_velocity_trajectory,
    saved_warmth_trajectory,
    control_porosity,
    control_volume_flag,
    entrance_face_flag,
):
    quadrature_factor = control_volume_flag.astype(jnp.float32)
    gamma = jnp.where(control_volume_flag == 1, control_porosity, jnp.float32(0.0))
    solid = 1.0 - gamma
    alpha = 3.0 * 0.1 * solid / (0.1 + gamma)
    porosity_sensitivity = -3.0 * 0.1 * 1.1 / ((0.1 + gamma) * (0.1 + gamma))
    leading_plane = lax.axis_index("space") == 0
    trailing_plane = lax.axis_index("space") == lax.axis_size("space") - 1
    device_instant_total = saved_warmth_trajectory.shape[0]
    cycle_ext = padded(saved_warmth_trajectory, (("space", 1),), 1)

    def closing_thermal_value(thermal_current_field, with_halo_padding):
        floor_limit = jnp.where(leading_plane, thermal_current_field[0], with_halo_padding[0])
        ceiling_bound = jnp.where(trailing_plane, thermal_current_field[-1], with_halo_padding[-1])
        return pad_sides(
            jnp.concatenate(
                [floor_limit[None], thermal_current_field, ceiling_bound[None]], axis=0
            ),
            "edge",
        )

    def one_step(adj, interior_block):
        speed = saved_velocity_trajectory[interior_block].astype(jnp.float32)
        thermal_current_field = saved_warmth_trajectory[interior_block].astype(jnp.float32)
        with_halo_padding = padded(adj, (("space", 1),), 1)
        thermal_halo_values = cycle_ext[interior_block].astype(jnp.float32)
        complete_thermal_field = jnp.concatenate(
            [thermal_halo_values[:1], thermal_current_field, thermal_halo_values[-1:]], axis=0
        )
        padded_thermal_field = closing_thermal_value(thermal_current_field, complete_thermal_field)
        ext_a = pad_sides(with_halo_padding[:3], "constant")
        current_adjoint_vector = adj[3]
        floor_limit = jnp.where(
            leading_plane,
            jnp.where(entrance_face_flag == 1, jnp.float32(0.0), current_adjoint_vector[0]),
            with_halo_padding[3, 0],
        )
        ceiling_bound = jnp.where(
            trailing_plane, current_adjoint_vector[-1], with_halo_padding[3, -1]
        )
        ext_b = pad_sides(
            jnp.concatenate(
                [floor_limit[None], current_adjoint_vector, ceiling_bound[None]], axis=0
            ),
            "edge",
        )
        return adjoint_update(
            adj,
            ext_a,
            ext_b,
            padded_thermal_field,
            speed,
            alpha,
            porosity_sensitivity,
            solid,
            quadrature_factor,
        )

    grid_shape = (4,) + control_porosity.shape
    adj = jnp.zeros(grid_shape, jnp.float32)
    for interior_block in range(device_instant_total - 1, -1, -1):
        adj, unused = one_step(adj, interior_block)
    adj = passed_along(adj, "arc", -1)
    partial_sum = jnp.zeros(control_porosity.shape, jnp.float32)
    for interior_block in range(device_instant_total - 1, -1, -1):
        adj, summand_contribution = one_step(adj, interior_block)
        partial_sum = partial_sum + summand_contribution
    summed = lax.psum(partial_sum, "arc")
    share = summed.shape[1] // lax.axis_size("arc")
    gradient = lax.dynamic_slice_in_dim(summed, lax.axis_index("arc") * share, share, 1)
    return (gradient, adj[None])


def solution(mesh):
    return jax.shard_map(
        body,
        mesh=mesh,
        in_specs=(
            P(("job", "arc"), None, "space", None, None),
            P(("job", "arc"), "space", None, None),
            P(("job", "space"), None, None),
            P(("job", "space"), None, None),
            P("job", None),
        ),
        out_specs=(P(("job", "space"), "arc", None), P(("job", "arc"), None, "space", None, None)),
        check_vma=False,
    )
```

profile of v0, /device:TPU:0, one launch (start us, length us, event | category | flops | bytes accessed | tf_op | source)
XLA Modules:
  0.0 265.9 jit_solution(15857158346192255144)
XLA Ops:
  9.4 3.8 %collective-permute-start.1 = (f32[4,1,128,128]{3,2,1,0:T(8,128)}, f32[4,1,128,128]{3,2,1,0:T(8,128)}, u32[]{:S(2)}, u32[]{:S(2)}) collective-permute-start(f32[4,1,128,128]{3,2,1,0:T(8,128)} %broadcast.302), channel_id=1, source_target_pairs={{0,4},{4,8},{8,12},{1,5},{5,9},{9,13},{2,6},{6,10},{10,14},{3,7},{... | collective-permute-start | bytes 786440 | tf_op jit(solution)/shard_map/ppermute | solution.py:15
  15.0 4.5 %collective-permute-start.2 = (bf16[8,1,128,128]{3,2,1,0:T(8,128)(2,1)}, bf16[8,1,128,128]{3,2,1,0:T(8,128)(2,1)}, u32[]{:S(2)}, u32[]{:S(2)}) collective-permute-start(bf16[8,1,128,128]{3,2,1,0:T(8,128)(2,1)} %get-tuple-element.84), channel_id=1, source_target_pairs={{0,4},{4,8},{8,12},{1,5},{5,9},{9,13},{2,6},{6,10},{10,14},{3,7},{... | collective-permute-start | bytes 786440 | tf_op jit(solution)/shard_map/ppermute | solution.py:15
  41.1 3.7 %collective-permute-start.5 = (f32[4,1,128,128]{3,2,1,0:T(8,128)S(1)}, f32[4,1,128,128]{3,2,1,0:T(8,128)S(1)}, u32[]{:S(2)}, u32[]{:S(2)}) collective-permute-start(f32[4,1,128,128]{3,2,1,0:T(8,128)S(1)} %get-tuple-element.81), channel_id=1, source_target_pairs={{0,4},{4,8},{8,12},{1,5},{5,9},{9,13},{2,6},{6,10},{10,14},{3,7},{... | collective-permute-start | bytes 786440 | tf_op jit(solution)/shard_map/ppermute | solution.py:15
  49.5 6.4 %collective-permute-start.7 = (f32[4,1,128,128]{3,2,1,0:T(8,128)S(1)}, f32[4,1,128,128]{3,2,1,0:T(8,128)S(1)}, u32[]{:S(2)}, u32[]{:S(2)}) collective-permute-start(f32[4,1,128,128]{3,2,1,0:T(8,128)S(1)} %get-tuple-element.79), channel_id=1, source_target_pairs={{0,4},{4,8},{8,12},{1,5},{5,9},{9,13},{2,6},{6,10},{10,14},{3,7},{... | collective-permute-start | bytes 786440 | tf_op jit(solution)/shard_map/ppermute | solution.py:15
  59.1 6.6 %collective-permute-start.9 = (f32[4,1,128,128]{3,2,1,0:T(8,128)S(1)}, f32[4,1,128,128]{3,2,1,0:T(8,128)S(1)}, u32[]{:S(2)}, u32[]{:S(2)}) collective-permute-start(f32[4,1,128,128]{3,2,1,0:T(8,128)S(1)} %get-tuple-element.77), channel_id=1, source_target_pairs={{0,4},{4,8},{8,12},{1,5},{5,9},{9,13},{2,6},{6,10},{10,14},{3,7},{... | collective-permute-start | bytes 786440 | tf_op jit(solution)/shard_map/ppermute | solution.py:15
  67.3 3.9 %collective-permute-done.8 = f32[4,1,128,128]{3,2,1,0:T(8,128)S(1)} collective-permute-done((f32[4,1,128,128]{3,2,1,0:T(8,128)S(1)}, f32[4,1,128,128]{3,2,1,0:T(8,128)S(1)}, u32[]{:S(2)}, u32[]{:S(2)}) %collective-permute-start.8) | collective-permute-done | bytes 262176 | tf_op jit(solution)/shard_map/ppermute | solution.py:17
  73.2 6.7 %collective-permute-start.11 = (f32[4,1,128,128]{3,2,1,0:T(8,128)S(1)}, f32[4,1,128,128]{3,2,1,0:T(8,128)S(1)}, u32[]{:S(2)}, u32[]{:S(2)}) collective-permute-start(f32[4,1,128,128]{3,2,1,0:T(8,128)S(1)} %get-tuple-element.75), channel_id=1, source_target_pairs={{0,4},{4,8},{8,12},{1,5},{5,9},{9,13},{2,6},{6,10},{10,14},{3,7},{... | collective-permute-start | bytes 786440 | tf_op jit(solution)/shard_map/ppermute | solution.py:15
  85.6 6.4 %collective-permute-start.13 = (f32[4,1,128,128]{3,2,1,0:T(8,128)S(1)}, f32[4,1,128,128]{3,2,1,0:T(8,128)S(1)}, u32[]{:S(2)}, u32[]{:S(2)}) collective-permute-start(f32[4,1,128,128]{3,2,1,0:T(8,128)S(1)} %get-tuple-element.73), channel_id=1, source_target_pairs={{0,4},{4,8},{8,12},{1,5},{5,9},{9,13},{2,6},{6,10},{10,14},{3,7},{... | collective-permute-start | bytes 786440 | tf_op jit(solution)/shard_map/ppermute | solution.py:15
  97.5 6.2 %collective-permute-start.15 = (f32[4,1,128,128]{3,2,1,0:T(8,128)S(1)}, f32[4,1,128,128]{3,2,1,0:T(8,128)S(1)}, u32[]{:S(2)}, u32[]{:S(2)}) collective-permute-start(f32[4,1,128,128]{3,2,1,0:T(8,128)S(1)} %get-tuple-element.71), channel_id=1, source_target_pairs={{0,4},{4,8},{8,12},{1,5},{5,9},{9,13},{2,6},{6,10},{10,14},{3,7},{... | collective-permute-start | bytes 786440 | tf_op jit(solution)/shard_map/ppermute | solution.py:15
  109.2 6.2 %collective-permute-start.17 = (f32[4,1,128,128]{3,2,1,0:T(8,128)S(1)}, f32[4,1,128,128]{3,2,1,0:T(8,128)S(1)}, u32[]{:S(2)}, u32[]{:S(2)}) collective-permute-start(f32[4,1,128,128]{3,2,1,0:T(8,128)S(1)} %get-tuple-element.69), channel_id=1, source_target_pairs={{0,4},{4,8},{8,12},{1,5},{5,9},{9,13},{2,6},{6,10},{10,14},{3,7},{... | collective-permute-start | bytes 786440 | tf_op jit(solution)/shard_map/ppermute | solution.py:15
  121.1 3.7 %collective-permute-start.18 = (f32[4,2,128,128]{3,2,1,0:T(8,128)S(1)}, f32[4,2,128,128]{3,2,1,0:T(8,128)S(1)}, u32[]{:S(2)}, u32[]{:S(2)}) collective-permute-start(f32[4,2,128,128]{3,2,1,0:T(8,128)S(1)} %pad_maximum_fusion.2), channel_id=1, source_target_pairs={{0,3},{1,0},{2,1},{3,2},{4,7},{5,4},{6,5},{7,6},{8,11},{9,8},{10,9... | collective-permute-start | bytes 1572872 | tf_op jit(solution)/shard_map/ppermute | solution.py:27
  124.8 9.0 %collective-permute-done.18 = f32[4,2,128,128]{3,2,1,0:T(8,128)S(1)} collective-permute-done((f32[4,2,128,128]{3,2,1,0:T(8,128)S(1)}, f32[4,2,128,128]{3,2,1,0:T(8,128)S(1)}, u32[]{:S(2)}, u32[]{:S(2)}) %collective-permute-start.18) | collective-permute-done | bytes 524320 | tf_op jit(solution)/shard_map/ppermute | solution.py:27
  133.8 5.3 %collective-permute-start.20 = (f32[4,1,128,128]{3,2,1,0:T(8,128)S(1)}, f32[4,1,128,128]{3,2,1,0:T(8,128)S(1)}, u32[]{:S(2)}, u32[]{:S(2)}) collective-permute-start(f32[4,1,128,128]{3,2,1,0:T(8,128)S(1)} %get-tuple-element.51), channel_id=1, source_target_pairs={{0,4},{4,8},{8,12},{1,5},{5,9},{9,13},{2,6},{6,10},{10,14},{3,7},{... | collective-permute-start | bytes 786440 | tf_op jit(solution)/shard_map/ppermute | solution.py:15
  144.1 6.2 %collective-permute-start.22 = (f32[4,1,128,128]{3,2,1,0:T(8,128)S(1)}, f32[4,1,128,128]{3,2,1,0:T(8,128)S(1)}, u32[]{:S(2)}, u32[]{:S(2)}) collective-permute-start(f32[4,1,128,128]{3,2,1,0:T(8,128)S(1)} %get-tuple-element.49), channel_id=1, source_target_pairs={{0,4},{4,8},{8,12},{1,5},{5,9},{9,13},{2,6},{6,10},{10,14},{3,7},{... | collective-permute-start | bytes 786440 | tf_op jit(solution)/shard_map/ppermute | solution.py:15
  151.7 2.1 collective-permute-done.21
  155.3 6.2 %collective-permute-start.24 = (f32[4,1,128,128]{3,2,1,0:T(8,128)S(1)}, f32[4,1,128,128]{3,2,1,0:T(8,128)S(1)}, u32[]{:S(2)}, u32[]{:S(2)}) collective-permute-start(f32[4,1,128,128]{3,2,1,0:T(8,128)S(1)} %get-tuple-element.47), channel_id=1, source_target_pairs={{0,4},{4,8},{8,12},{1,5},{5,9},{9,13},{2,6},{6,10},{10,14},{3,7},{... | collective-permute-start | bytes 786440 | tf_op jit(solution)/shard_map/ppermute | solution.py:15
  162.8 2.1 collective-permute-done.23
  166.4 6.2 %collective-permute-start.26 = (f32[4,1,128,128]{3,2,1,0:T(8,128)S(1)}, f32[4,1,128,128]{3,2,1,0:T(8,128)S(1)}, u32[]{:S(2)}, u32[]{:S(2)}) collective-permute-start(f32[4,1,128,128]{3,2,1,0:T(8,128)S(1)} %get-tuple-element.45), channel_id=1, source_target_pairs={{0,4},{4,8},{8,12},{1,5},{5,9},{9,13},{2,6},{6,10},{10,14},{3,7},{... | collective-permute-start | bytes 786440 | tf_op jit(solution)/shard_map/ppermute | solution.py:15
  177.6 6.2 %collective-permute-start.28 = (f32[4,1,128,128]{3,2,1,0:T(8,128)S(1)}, f32[4,1,128,128]{3,2,1,0:T(8,128)S(1)}, u32[]{:S(2)}, u32[]{:S(2)}) collective-permute-start(f32[4,1,128,128]{3,2,1,0:T(8,128)S(1)} %get-tuple-element.43), channel_id=1, source_target_pairs={{0,4},{4,8},{8,12},{1,5},{5,9},{9,13},{2,6},{6,10},{10,14},{3,7},{... | collective-permute-start | bytes 786440 | tf_op jit(solution)/shard_map/ppermute | solution.py:15
  188.7 6.2 %collective-permute-start.30 = (f32[4,1,128,128]{3,2,1,0:T(8,128)S(1)}, f32[4,1,128,128]{3,2,1,0:T(8,128)S(1)}, u32[]{:S(2)}, u32[]{:S(2)}) collective-permute-start(f32[4,1,128,128]{3,2,1,0:T(8,128)S(1)} %get-tuple-element.41), channel_id=1, source_target_pairs={{0,4},{4,8},{8,12},{1,5},{5,9},{9,13},{2,6},{6,10},{10,14},{3,7},{... | collective-permute-start | bytes 786440 | tf_op jit(solution)/shard_map/ppermute | solution.py:15
  199.8 6.2 %collective-permute-start.32 = (f32[4,1,128,128]{3,2,1,0:T(8,128)S(1)}, f32[4,1,128,128]{3,2,1,0:T(8,128)S(1)}, u32[]{:S(2)}, u32[]{:S(2)}) collective-permute-start(f32[4,1,128,128]{3,2,1,0:T(8,128)S(1)} %get-tuple-element.39), channel_id=1, source_target_pairs={{0,4},{4,8},{8,12},{1,5},{5,9},{9,13},{2,6},{6,10},{10,14},{3,7},{... | collective-permute-start | bytes 786440 | tf_op jit(solution)/shard_map/ppermute | solution.py:15
  207.4 2.1 collective-permute-done.31
  213.1 6.2 %collective-permute-start.34 = (f32[4,1,128,128]{3,2,1,0:T(8,128)S(1)}, f32[4,1,128,128]{3,2,1,0:T(8,128)S(1)}, u32[]{:S(2)}, u32[]{:S(2)}) collective-permute-start(f32[4,1,128,128]{3,2,1,0:T(8,128)S(1)} %get-tuple-element.37), channel_id=1, source_target_pairs={{0,4},{4,8},{8,12},{1,5},{5,9},{9,13},{2,6},{6,10},{10,14},{3,7},{... | collective-permute-start | bytes 786440 | tf_op jit(solution)/shard_map/ppermute | solution.py:15
  220.6 34.2 %all-reduce.22.cloned.1.call-done = f32[2,128,128]{2,1,0:T(8,128)} async-done(((f32[2,128,128]{2,1,0:T(8,128)}), f32[2,128,128]{2,1,0:T(8,128)}) %all-reduce.22.cloned.1.call-update) | async-done | bytes 131088 | tf_op jit(solution)/shard_map/psum | solution.py:162
  (379 shorter events, 93.8 us)
Async XLA Ops:
  7.2 247.6 %all-reduce.22.cloned.1.call-start = ((), (), s32[]{:S(2)}) async-start(), calls=%async_computation | async-start | bytes 262144 | tf_op jit(solution)/shard_map/psum | solution.py:162
  8.0 27.7 %collective-permute-start = (f32[4,1,128,128]{3,2,1,0:T(8,128)}, f32[4,1,128,128]{3,2,1,0:T(8,128)}, u32[]{:S(2)}, u32[]{:S(2)}) collective-permute-start(f32[4,1,128,128]{3,2,1,0:T(8,128)} %broadcast.302), channel_id=1, source_target_pairs={{4,0},{8,4},{12,8},{5,1},{9,5},{13,9},{6,2},{10,6},{14,10},{7,3},{... | collective-permute-start | bytes 786440 | tf_op jit(solution)/shard_map/ppermute | solution.py:17
  9.4 25.2 %collective-permute-start.1 = (f32[4,1,128,128]{3,2,1,0:T(8,128)}, f32[4,1,128,128]{3,2,1,0:T(8,128)}, u32[]{:S(2)}, u32[]{:S(2)}) collective-permute-start(f32[4,1,128,128]{3,2,1,0:T(8,128)} %broadcast.302), channel_id=1, source_target_pairs={{0,4},{4,8},{8,12},{1,5},{5,9},{9,13},{2,6},{6,10},{10,14},{3,7},{... | collective-permute-start | bytes 786440 | tf_op jit(solution)/shard_map/ppermute | solution.py:15
  15.0 13.9 %collective-permute-start.2 = (bf16[8,1,128,128]{3,2,1,0:T(8,128)(2,1)}, bf16[8,1,128,128]{3,2,1,0:T(8,128)(2,1)}, u32[]{:S(2)}, u32[]{:S(2)}) collective-permute-start(bf16[8,1,128,128]{3,2,1,0:T(8,128)(2,1)} %get-tuple-element.84), channel_id=1, source_target_pairs={{0,4},{4,8},{8,12},{1,5},{5,9},{9,13},{2,6},{6,10},{10,14},{3,7},{... | collective-permute-start | bytes 786440 | tf_op jit(solution)/shard_map/ppermute | solution.py:15
  19.5 10.5 %collective-permute-start.3 = (bf16[8,1,128,128]{3,2,1,0:T(8,128)(2,1)}, bf16[8,1,128,128]{3,2,1,0:T(8,128)(2,1)}, u32[]{:S(2)}, u32[]{:S(2)}) collective-permute-start(bf16[8,1,128,128]{3,2,1,0:T(8,128)(2,1)} %get-tuple-element.83), channel_id=1, source_target_pairs={{4,0},{8,4},{12,8},{5,1},{9,5},{13,9},{6,2},{10,6},{14,10},{7,3},{... | collective-permute-start | bytes 786440 | tf_op jit(solution)/shard_map/ppermute | solution.py:17
  39.8 5.3 %collective-permute-start.4 = (f32[4,1,128,128]{3,2,1,0:T(8,128)S(1)}, f32[4,1,128,128]{3,2,1,0:T(8,128)S(1)}, u32[]{:S(2)}, u32[]{:S(2)}) collective-permute-start(f32[4,1,128,128]{3,2,1,0:T(8,128)S(1)} %get-tuple-element.82), channel_id=1, source_target_pairs={{4,0},{8,4},{12,8},{5,1},{9,5},{13,9},{6,2},{10,6},{14,10},{7,3},{... | collective-permute-start | bytes 786440 | tf_op jit(solution)/shard_map/ppermute | solution.py:17
  48.1 8.0 %collective-permute-start.6 = (f32[4,1,128,128]{3,2,1,0:T(8,128)S(1)}, f32[4,1,128,128]{3,2,1,0:T(8,128)S(1)}, u32[]{:S(2)}, u32[]{:S(2)}) collective-permute-start(f32[4,1,128,128]{3,2,1,0:T(8,128)S(1)} %get-tuple-element.80), channel_id=1, source_target_pairs={{4,0},{8,4},{12,8},{5,1},{9,5},{13,9},{6,2},{10,6},{14,10},{7,3},{... | collective-permute-start | bytes 786440 | tf_op jit(solution)/shard_map/ppermute | solution.py:17
  49.5 7.6 %collective-permute-start.7 = (f32[4,1,128,128]{3,2,1,0:T(8,128)S(1)}, f32[4,1,128,128]{3,2,1,0:T(8,128)S(1)}, u32[]{:S(2)}, u32[]{:S(2)}) collective-permute-start(f32[4,1,128,128]{3,2,1,0:T(8,128)S(1)} %get-tuple-element.79), channel_id=1, source_target_pairs={{0,4},{4,8},{8,12},{1,5},{5,9},{9,13},{2,6},{6,10},{10,14},{3,7},{... | collective-permute-start | bytes 786440 | tf_op jit(solution)/shard_map/ppermute | solution.py:15
  59.1 8.1 %collective-permute-start.9 = (f32[4,1,128,128]{3,2,1,0:T(8,128)S(1)}, f32[4,1,128,128]{3,2,1,0:T(8,128)S(1)}, u32[]{:S(2)}, u32[]{:S(2)}) collective-permute-start(f32[4,1,128,128]{3,2,1,0:T(8,128)S(1)} %get-tuple-element.77), channel_id=1, source_target_pairs={{0,4},{4,8},{8,12},{1,5},{5,9},{9,13},{2,6},{6,10},{10,14},{3,7},{... | collective-permute-start | bytes 786440 | tf_op jit(solution)/shard_map/ppermute | solution.py:15
  65.8 5.4 %collective-permute-start.8 = (f32[4,1,128,128]{3,2,1,0:T(8,128)S(1)}, f32[4,1,128,128]{3,2,1,0:T(8,128)S(1)}, u32[]{:S(2)}, u32[]{:S(2)}) collective-permute-start(f32[4,1,128,128]{3,2,1,0:T(8,128)S(1)} %get-tuple-element.78), channel_id=1, source_target_pairs={{4,0},{8,4},{12,8},{5,1},{9,5},{13,9},{6,2},{10,6},{14,10},{7,3},{... | collective-permute-start | bytes 786440 | tf_op jit(solution)/shard_map/ppermute | solution.py:17
  73.2 8.4 %collective-permute-start.11 = (f32[4,1,128,128]{3,2,1,0:T(8,128)S(1)}, f32[4,1,128,128]{3,2,1,0:T(8,128)S(1)}, u32[]{:S(2)}, u32[]{:S(2)}) collective-permute-start(f32[4,1,128,128]{3,2,1,0:T(8,128)S(1)} %get-tuple-element.75), channel_id=1, source_target_pairs={{0,4},{4,8},{8,12},{1,5},{5,9},{9,13},{2,6},{6,10},{10,14},{3,7},{... | collective-permute-start | bytes 786440 | tf_op jit(solution)/shard_map/ppermute | solution.py:15
  85.6 8.0 %collective-permute-start.13 = (f32[4,1,128,128]{3,2,1,0:T(8,128)S(1)}, f32[4,1,128,128]{3,2,1,0:T(8,128)S(1)}, u32[]{:S(2)}, u32[]{:S(2)}) collective-permute-start(f32[4,1,128,128]{3,2,1,0:T(8,128)S(1)} %get-tuple-element.73), channel_id=1, source_target_pairs={{0,4},{4,8},{8,12},{1,5},{5,9},{9,13},{2,6},{6,10},{10,14},{3,7},{... | collective-permute-start | bytes 786440 | tf_op jit(solution)/shard_map/ppermute | solution.py:15
  97.5 7.7 %collective-permute-start.15 = (f32[4,1,128,128]{3,2,1,0:T(8,128)S(1)}, f32[4,1,128,128]{3,2,1,0:T(8,128)S(1)}, u32[]{:S(2)}, u32[]{:S(2)}) collective-permute-start(f32[4,1,128,128]{3,2,1,0:T(8,128)S(1)} %get-tuple-element.71), channel_id=1, source_target_pairs={{0,4},{4,8},{8,12},{1,5},{5,9},{9,13},{2,6},{6,10},{10,14},{3,7},{... | collective-permute-start | bytes 786440 | tf_op jit(solution)/shard_map/ppermute | solution.py:15
  109.2 7.9 %collective-permute-start.17 = (f32[4,1,128,128]{3,2,1,0:T(8,128)S(1)}, f32[4,1,128,128]{3,2,1,0:T(8,128)S(1)}, u32[]{:S(2)}, u32[]{:S(2)}) collective-permute-start(f32[4,1,128,128]{3,2,1,0:T(8,128)S(1)} %get-tuple-element.69), channel_id=1, source_target_pairs={{0,4},{4,8},{8,12},{1,5},{5,9},{9,13},{2,6},{6,10},{10,14},{3,7},{... | collective-permute-start | bytes 786440 | tf_op jit(solution)/shard_map/ppermute | solution.py:15
  121.1 12.7 %collective-permute-start.18 = (f32[4,2,128,128]{3,2,1,0:T(8,128)S(1)}, f32[4,2,128,128]{3,2,1,0:T(8,128)S(1)}, u32[]{:S(2)}, u32[]{:S(2)}) collective-permute-start(f32[4,2,128,128]{3,2,1,0:T(8,128)S(1)} %pad_maximum_fusion.2), channel_id=1, source_target_pairs={{0,3},{1,0},{2,1},{3,2},{4,7},{5,4},{6,5},{7,6},{8,11},{9,8},{10,9... | collective-permute-start | bytes 1572872 | tf_op jit(solution)/shard_map/ppermute | solution.py:27
  133.8 6.7 %collective-permute-start.20 = (f32[4,1,128,128]{3,2,1,0:T(8,128)S(1)}, f32[4,1,128,128]{3,2,1,0:T(8,128)S(1)}, u32[]{:S(2)}, u32[]{:S(2)}) collective-permute-start(f32[4,1,128,128]{3,2,1,0:T(8,128)S(1)} %get-tuple-element.51), channel_id=1, source_target_pairs={{0,4},{4,8},{8,12},{1,5},{5,9},{9,13},{2,6},{6,10},{10,14},{3,7},{... | collective-permute-start | bytes 786440 | tf_op jit(solution)/shard_map/ppermute | solution.py:15
  144.1 7.5 %collective-permute-start.22 = (f32[4,1,128,128]{3,2,1,0:T(8,128)S(1)}, f32[4,1,128,128]{3,2,1,0:T(8,128)S(1)}, u32[]{:S(2)}, u32[]{:S(2)}) collective-permute-start(f32[4,1,128,128]{3,2,1,0:T(8,128)S(1)} %get-tuple-element.49), channel_id=1, source_target_pairs={{0,4},{4,8},{8,12},{1,5},{5,9},{9,13},{2,6},{6,10},{10,14},{3,7},{... | collective-permute-start | bytes 786440 | tf_op jit(solution)/shard_map/ppermute | solution.py:15
  155.3 7.5 %collective-permute-start.24 = (f32[4,1,128,128]{3,2,1,0:T(8,128)S(1)}, f32[4,1,128,128]{3,2,1,0:T(8,128)S(1)}, u32[]{:S(2)}, u32[]{:S(2)}) collective-permute-start(f32[4,1,128,128]{3,2,1,0:T(8,128)S(1)} %get-tuple-element.47), channel_id=1, source_target_pairs={{0,4},{4,8},{8,12},{1,5},{5,9},{9,13},{2,6},{6,10},{10,14},{3,7},{... | collective-permute-start | bytes 786440 | tf_op jit(solution)/shard_map/ppermute | solution.py:15
  166.4 7.7 %collective-permute-start.26 = (f32[4,1,128,128]{3,2,1,0:T(8,128)S(1)}, f32[4,1,128,128]{3,2,1,0:T(8,128)S(1)}, u32[]{:S(2)}, u32[]{:S(2)}) collective-permute-start(f32[4,1,128,128]{3,2,1,0:T(8,128)S(1)} %get-tuple-element.45), channel_id=1, source_target_pairs={{0,4},{4,8},{8,12},{1,5},{5,9},{9,13},{2,6},{6,10},{10,14},{3,7},{... | collective-permute-start | bytes 786440 | tf_op jit(solution)/shard_map/ppermute | solution.py:15
  177.6 7.5 %collective-permute-start.28 = (f32[4,1,128,128]{3,2,1,0:T(8,128)S(1)}, f32[4,1,128,128]{3,2,1,0:T(8,128)S(1)}, u32[]{:S(2)}, u32[]{:S(2)}) collective-permute-start(f32[4,1,128,128]{3,2,1,0:T(8,128)S(1)} %get-tuple-element.43), channel_id=1, source_target_pairs={{0,4},{4,8},{8,12},{1,5},{5,9},{9,13},{2,6},{6,10},{10,14},{3,7},{... | collective-permute-start | bytes 786440 | tf_op jit(solution)/shard_map/ppermute | solution.py:15
  188.7 7.5 %collective-permute-start.30 = (f32[4,1,128,128]{3,2,1,0:T(8,128)S(1)}, f32[4,1,128,128]{3,2,1,0:T(8,128)S(1)}, u32[]{:S(2)}, u32[]{:S(2)}) collective-permute-start(f32[4,1,128,128]{3,2,1,0:T(8,128)S(1)} %get-tuple-element.41), channel_id=1, source_target_pairs={{0,4},{4,8},{8,12},{1,5},{5,9},{9,13},{2,6},{6,10},{10,14},{3,7},{... | collective-permute-start | bytes 786440 | tf_op jit(solution)/shard_map/ppermute | solution.py:15
  199.8 7.5 %collective-permute-start.32 = (f32[4,1,128,128]{3,2,1,0:T(8,128)S(1)}, f32[4,1,128,128]{3,2,1,0:T(8,128)S(1)}, u32[]{:S(2)}, u32[]{:S(2)}) collective-permute-start(f32[4,1,128,128]{3,2,1,0:T(8,128)S(1)} %get-tuple-element.39), channel_id=1, source_target_pairs={{0,4},{4,8},{8,12},{1,5},{5,9},{9,13},{2,6},{6,10},{10,14},{3,7},{... | collective-permute-start | bytes 786440 | tf_op jit(solution)/shard_map/ppermute | solution.py:15
  213.1 43.1 %collective-permute-start.34 = (f32[4,1,128,128]{3,2,1,0:T(8,128)S(1)}, f32[4,1,128,128]{3,2,1,0:T(8,128)S(1)}, u32[]{:S(2)}, u32[]{:S(2)}) collective-permute-start(f32[4,1,128,128]{3,2,1,0:T(8,128)S(1)} %get-tuple-element.37), channel_id=1, source_target_pairs={{0,4},{4,8},{8,12},{1,5},{5,9},{9,13},{2,6},{6,10},{10,14},{3,7},{... | collective-permute-start | bytes 786440 | tf_op jit(solution)/shard_map/ppermute | solution.py:15
  219.3 36.9 %collective-permute-start.33 = (f32[4,1,128,128]{3,2,1,0:T(8,128)S(1)}, f32[4,1,128,128]{3,2,1,0:T(8,128)S(1)}, u32[]{:S(2)}, u32[]{:S(2)}) collective-permute-start(f32[4,1,128,128]{3,2,1,0:T(8,128)S(1)} %get-tuple-element.38), channel_id=1, source_target_pairs={{4,0},{8,4},{12,8},{5,1},{9,5},{13,9},{6,2},{10,6},{14,10},{7,3},{... | collective-permute-start | bytes 786440 | tf_op jit(solution)/shard_map/ppermute | solution.py:17
  (71 other events, 174.1 us)
Sparse Core Ops, SparseCore 0:
  219.4 35.3 all-reduce.21
where the time goes:
time: 267 us; the launch traced here: 266 us
  starting transfers between devices  125 us (47%)
  waiting for transfers between devices  71 us (27%)
  other arithmetic  37.5 us (14%)
  local copies, waits for them, and re-layouts  16.4 us (6%)
  between operations  16.1 us (6%)
    ppermute x17, starting transfers between devices, padded(): lax.ppermute(tail, axis, [(i, (i + 1) % count) for i in range(ends)])  99 us
    psum x1, waiting for transfers between devices, body(): summed = lax.psum(partial_sum, 'arc')  34.2 us
    ppermute x17, waiting for transfers between devices, padded(): lax.ppermute(head, axis, [((i + 1) % count, i) for i in range(ends)])  26 us
    ppermute x17, starting transfers between devices, padded(): lax.ppermute(head, axis, [((i + 1) % count, i) for i in range(ends)])  22.3 us
    ppermute x1, waiting for transfers between devices, passed_along(): return lax.ppermute(value, axis, pairs)  9.02 us
    concatenate x16, other arithmetic, padded(): jnp.concatenate([lax.ppermute(tail, axis, [(i, (i + 1) % count) for i in...  8.71 us
    unnamed x120, local copies, waits for them, and re-layouts  8.05 us
    add x14, other arithmetic, adjoint_update(): a_now + 0.1 * (1.2 * laplace(ext_a) + carry_a - alpha * a_now - current_a...  7.44 us
  transfers between devices with their start and end apart: 36, of which 16 were waited for; matrix products, arithmetic and copies ran while one was open for 7% of the time, Pallas kernels for 0%

commit v1 on v0

--- a/solution.py
+++ b/solution.py
@@ -1,7 +1,23 @@
+import functools
 import jax
 import jax.numpy as jnp
 from jax import lax
 from jax.sharding import PartitionSpec as P
+
+
+def _store_task(array_here, across):
+    m_next, e_now = (array_here, 0)
+    chips = lax.axis_size(across)
+    while 1 << e_now < chips:
+        s_next = lax.ppermute(
+            m_next, across, list(map(lambda nth: (nth, nth ^ 1 << e_now), range(chips)))
+        )
+        m_next = m_next + s_next
+        e_now = e_now + 1
+    return m_next
+
+
+obtain_target_on = functools.partial(_store_task, across="arc")
 
 
 def padded(cells, sides, width):
@@ -159,7 +175,7 @@
     for interior_block in range(device_instant_total - 1, -1, -1):
         adj, summand_contribution = one_step(adj, interior_block)
         partial_sum = partial_sum + summand_contribution
-    summed = lax.psum(partial_sum, "arc")
+    summed = obtain_target_on(partial_sum)
     share = summed.shape[1] // lax.axis_size("arc")
     gradient = lax.dynamic_slice_in_dim(summed, lax.axis_index("arc") * share, share, 1)
     return (gradient, adj[None])

time: 267 us -> 228 us (0.85)
  waiting for transfers between devices: 71 us -> 43.9 us
  between operations: 16.1 us -> 2.68 us
  starting transfers between devices: 125 us -> 128 us
    psum x1 -> x0, waiting for transfers between devices: 34.2 us -> none  [body(): summed = lax.psum(partial_sum, 'arc')]
    ppermute x0 -> x2, waiting for transfers between devices: none -> 7.06 us  [_store_task(): lax.ppermute(m_next, across, list(map(lambda nth: (nth, nth ^ 1 << e_now)...]
    ppermute x0 -> x2, starting transfers between devices: none -> 3.1 us  [_store_task(): lax.ppermute(m_next, across, list(map(lambda nth: (nth, nth ^ 1 << e_now)...]
  transfers between devices with their start and end apart: 36 -> 37, of which waited for: 16 -> 17; matrix products, arithmetic and copies ran while one was open for 7% -> 8% of each run, Pallas kernels for 0% -> 0%
where the time goes in v1:
time: 228 us; the launch traced here: 227 us
  starting transfers between devices  128 us (56%)
  waiting for transfers between devices  43.9 us (19%)
  other arithmetic  37.4 us (16%)
  local copies, waits for them, and re-layouts  14.9 us (7%)
  between operations  2.68 us (1%)
    ppermute x17, starting transfers between devices, padded(): lax.ppermute(tail, axis, [(i, (i + 1) % count) for i in range(ends)])  98.8 us
    ppermute x17, waiting for transfers between devices, padded(): lax.ppermute(head, axis, [((i + 1) % count, i) for i in range(ends)])  26 us
    ppermute x17, starting transfers between devices, padded(): lax.ppermute(head, axis, [((i + 1) % count, i) for i in range(ends)])  22.5 us
    ppermute x1, waiting for transfers between devices, passed_along(): return lax.ppermute(value, axis, pairs)  9.02 us
    concatenate x16, other arithmetic, padded(): jnp.concatenate([lax.ppermute(tail, axis, [(i, (i + 1) % count) for i in...  8.72 us
    unnamed x120, local copies, waits for them, and re-layouts  7.9 us
    add x14, other arithmetic, adjoint_update(): a_now + 0.1 * (1.2 * laplace(ext_a) + carry_a - alpha * a_now - current_a...  7.44 us
    ppermute x2, waiting for transfers between devices, _store_task(): lax.ppermute(m_next, across, list(map(lambda nth: (nth, nth ^ 1 << e_now)...  7.06 us
  transfers between devices with their start and end apart: 37, of which 17 were waited for; matrix products, arithmetic and copies ran while one was open for 8% of the time, Pallas kernels for 0%

profile of v1, /device:TPU:0, one launch (start us, length us, event | category | flops | bytes accessed | tf_op | source)
XLA Modules:
  0.0 226.8 jit_solution(4099403826834384544)
XLA Ops:
  2.8 3.7 %collective-permute-start.1 = (f32[4,1,128,128]{3,2,1,0:T(8,128)}, f32[4,1,128,128]{3,2,1,0:T(8,128)}, u32[]{:S(2)}, u32[]{:S(2)}) collective-permute-start(f32[4,1,128,128]{3,2,1,0:T(8,128)} %broadcast.302), channel_id=1, source_target_pairs={{0,4},{4,8},{8,12},{1,5},{5,9},{9,13},{2,6},{6,10},{10,14},{3,7},{... | collective-permute-start | bytes 786440 | tf_op jit(solution)/shard_map/ppermute | solution.py:31
  8.4 4.5 %collective-permute-start.2 = (bf16[8,1,128,128]{3,2,1,0:T(8,128)(2,1)}, bf16[8,1,128,128]{3,2,1,0:T(8,128)(2,1)}, u32[]{:S(2)}, u32[]{:S(2)}) collective-permute-start(bf16[8,1,128,128]{3,2,1,0:T(8,128)(2,1)} %get-tuple-element.84), channel_id=1, source_target_pairs={{0,4},{4,8},{8,12},{1,5},{5,9},{9,13},{2,6},{6,10},{10,14},{3,7},{... | collective-permute-start | bytes 786440 | tf_op jit(solution)/shard_map/ppermute | solution.py:31
  34.4 3.7 %collective-permute-start.5 = (f32[4,1,128,128]{3,2,1,0:T(8,128)S(1)}, f32[4,1,128,128]{3,2,1,0:T(8,128)S(1)}, u32[]{:S(2)}, u32[]{:S(2)}) collective-permute-start(f32[4,1,128,128]{3,2,1,0:T(8,128)S(1)} %get-tuple-element.81), channel_id=1, source_target_pairs={{0,4},{4,8},{8,12},{1,5},{5,9},{9,13},{2,6},{6,10},{10,14},{3,7},{... | collective-permute-start | bytes 786440 | tf_op jit(solution)/shard_map/ppermute | solution.py:31
  42.8 6.4 %collective-permute-start.7 = (f32[4,1,128,128]{3,2,1,0:T(8,128)S(1)}, f32[4,1,128,128]{3,2,1,0:T(8,128)S(1)}, u32[]{:S(2)}, u32[]{:S(2)}) collective-permute-start(f32[4,1,128,128]{3,2,1,0:T(8,128)S(1)} %get-tuple-element.79), channel_id=1, source_target_pairs={{0,4},{4,8},{8,12},{1,5},{5,9},{9,13},{2,6},{6,10},{10,14},{3,7},{... | collective-permute-start | bytes 786440 | tf_op jit(solution)/shard_map/ppermute | solution.py:31
  52.4 6.6 %collective-permute-start.9 = (f32[4,1,128,128]{3,2,1,0:T(8,128)S(1)}, f32[4,1,128,128]{3,2,1,0:T(8,128)S(1)}, u32[]{:S(2)}, u32[]{:S(2)}) collective-permute-start(f32[4,1,128,128]{3,2,1,0:T(8,128)S(1)} %get-tuple-element.77), channel_id=1, source_target_pairs={{0,4},{4,8},{8,12},{1,5},{5,9},{9,13},{2,6},{6,10},{10,14},{3,7},{... | collective-permute-start | bytes 786440 | tf_op jit(solution)/shard_map/ppermute | solution.py:31
  60.6 3.9 %collective-permute-done.8 = f32[4,1,128,128]{3,2,1,0:T(8,128)S(1)} collective-permute-done((f32[4,1,128,128]{3,2,1,0:T(8,128)S(1)}, f32[4,1,128,128]{3,2,1,0:T(8,128)S(1)}, u32[]{:S(2)}, u32[]{:S(2)}) %collective-permute-start.8) | collective-permute-done | bytes 262176 | tf_op jit(solution)/shard_map/ppermute | solution.py:33
  66.5 6.7 %collective-permute-start.11 = (f32[4,1,128,128]{3,2,1,0:T(8,128)S(1)}, f32[4,1,128,128]{3,2,1,0:T(8,128)S(1)}, u32[]{:S(2)}, u32[]{:S(2)}) collective-permute-start(f32[4,1,128,128]{3,2,1,0:T(8,128)S(1)} %get-tuple-element.75), channel_id=1, source_target_pairs={{0,4},{4,8},{8,12},{1,5},{5,9},{9,13},{2,6},{6,10},{10,14},{3,7},{... | collective-permute-start | bytes 786440 | tf_op jit(solution)/shard_map/ppermute | solution.py:31
  78.9 6.2 %collective-permute-start.13 = (f32[4,1,128,128]{3,2,1,0:T(8,128)S(1)}, f32[4,1,128,128]{3,2,1,0:T(8,128)S(1)}, u32[]{:S(2)}, u32[]{:S(2)}) collective-permute-start(f32[4,1,128,128]{3,2,1,0:T(8,128)S(1)} %get-tuple-element.73), channel_id=1, source_target_pairs={{0,4},{4,8},{8,12},{1,5},{5,9},{9,13},{2,6},{6,10},{10,14},{3,7},{... | collective-permute-start | bytes 786440 | tf_op jit(solution)/shard_map/ppermute | solution.py:31
  90.8 6.2 %collective-permute-start.15 = (f32[4,1,128,128]{3,2,1,0:T(8,128)S(1)}, f32[4,1,128,128]{3,2,1,0:T(8,128)S(1)}, u32[]{:S(2)}, u32[]{:S(2)}) collective-permute-start(f32[4,1,128,128]{3,2,1,0:T(8,128)S(1)} %get-tuple-element.71), channel_id=1, source_target_pairs={{0,4},{4,8},{8,12},{1,5},{5,9},{9,13},{2,6},{6,10},{10,14},{3,7},{... | collective-permute-start | bytes 786440 | tf_op jit(solution)/shard_map/ppermute | solution.py:31
  102.5 6.2 %collective-permute-start.17 = (f32[4,1,128,128]{3,2,1,0:T(8,128)S(1)}, f32[4,1,128,128]{3,2,1,0:T(8,128)S(1)}, u32[]{:S(2)}, u32[]{:S(2)}) collective-permute-start(f32[4,1,128,128]{3,2,1,0:T(8,128)S(1)} %get-tuple-element.69), channel_id=1, source_target_pairs={{0,4},{4,8},{8,12},{1,5},{5,9},{9,13},{2,6},{6,10},{10,14},{3,7},{... | collective-permute-start | bytes 786440 | tf_op jit(solution)/shard_map/ppermute | solution.py:31
  114.4 3.7 %collective-permute-start.18 = (f32[4,2,128,128]{3,2,1,0:T(8,128)S(1)}, f32[4,2,128,128]{3,2,1,0:T(8,128)S(1)}, u32[]{:S(2)}, u32[]{:S(2)}) collective-permute-start(f32[4,2,128,128]{3,2,1,0:T(8,128)S(1)} %pad_maximum_fusion.2), channel_id=1, source_target_pairs={{0,3},{1,0},{2,1},{3,2},{4,7},{5,4},{6,5},{7,6},{8,11},{9,8},{10,9... | collective-permute-start | bytes 1572872 | tf_op jit(solution)/shard_map/ppermute | solution.py:43
  118.1 9.0 %collective-permute-done.18 = f32[4,2,128,128]{3,2,1,0:T(8,128)S(1)} collective-permute-done((f32[4,2,128,128]{3,2,1,0:T(8,128)S(1)}, f32[4,2,128,128]{3,2,1,0:T(8,128)S(1)}, u32[]{:S(2)}, u32[]{:S(2)}) %collective-permute-start.18) | collective-permute-done | bytes 524320 | tf_op jit(solution)/shard_map/ppermute | solution.py:43
  127.1 5.3 %collective-permute-start.20 = (f32[4,1,128,128]{3,2,1,0:T(8,128)S(1)}, f32[4,1,128,128]{3,2,1,0:T(8,128)S(1)}, u32[]{:S(2)}, u32[]{:S(2)}) collective-permute-start(f32[4,1,128,128]{3,2,1,0:T(8,128)S(1)} %get-tuple-element.51), channel_id=1, source_target_pairs={{0,4},{4,8},{8,12},{1,5},{5,9},{9,13},{2,6},{6,10},{10,14},{3,7},{... | collective-permute-start | bytes 786440 | tf_op jit(solution)/shard_map/ppermute | solution.py:31
  137.4 6.2 %collective-permute-start.22 = (f32[4,1,128,128]{3,2,1,0:T(8,128)S(1)}, f32[4,1,128,128]{3,2,1,0:T(8,128)S(1)}, u32[]{:S(2)}, u32[]{:S(2)}) collective-permute-start(f32[4,1,128,128]{3,2,1,0:T(8,128)S(1)} %get-tuple-element.49), channel_id=1, source_target_pairs={{0,4},{4,8},{8,12},{1,5},{5,9},{9,13},{2,6},{6,10},{10,14},{3,7},{... | collective-permute-start | bytes 786440 | tf_op jit(solution)/shard_map/ppermute | solution.py:31
  144.9 2.1 collective-permute-done.21
  148.6 6.2 %collective-permute-start.24 = (f32[4,1,128,128]{3,2,1,0:T(8,128)S(1)}, f32[4,1,128,128]{3,2,1,0:T(8,128)S(1)}, u32[]{:S(2)}, u32[]{:S(2)}) collective-permute-start(f32[4,1,128,128]{3,2,1,0:T(8,128)S(1)} %get-tuple-element.47), channel_id=1, source_target_pairs={{0,4},{4,8},{8,12},{1,5},{5,9},{9,13},{2,6},{6,10},{10,14},{3,7},{... | collective-permute-start | bytes 786440 | tf_op jit(solution)/shard_map/ppermute | solution.py:31
  159.7 6.2 %collective-permute-start.26 = (f32[4,1,128,128]{3,2,1,0:T(8,128)S(1)}, f32[4,1,128,128]{3,2,1,0:T(8,128)S(1)}, u32[]{:S(2)}, u32[]{:S(2)}) collective-permute-start(f32[4,1,128,128]{3,2,1,0:T(8,128)S(1)} %get-tuple-element.45), channel_id=1, source_target_pairs={{0,4},{4,8},{8,12},{1,5},{5,9},{9,13},{2,6},{6,10},{10,14},{3,7},{... | collective-permute-start | bytes 786440 | tf_op jit(solution)/shard_map/ppermute | solution.py:31
  170.9 6.2 %collective-permute-start.28 = (f32[4,1,128,128]{3,2,1,0:T(8,128)S(1)}, f32[4,1,128,128]{3,2,1,0:T(8,128)S(1)}, u32[]{:S(2)}, u32[]{:S(2)}) collective-permute-start(f32[4,1,128,128]{3,2,1,0:T(8,128)S(1)} %get-tuple-element.43), channel_id=1, source_target_pairs={{0,4},{4,8},{8,12},{1,5},{5,9},{9,13},{2,6},{6,10},{10,14},{3,7},{... | collective-permute-start | bytes 786440 | tf_op jit(solution)/shard_map/ppermute | solution.py:31
  182.0 6.2 %collective-permute-start.30 = (f32[4,1,128,128]{3,2,1,0:T(8,128)S(1)}, f32[4,1,128,128]{3,2,1,0:T(8,128)S(1)}, u32[]{:S(2)}, u32[]{:S(2)}) collective-permute-start(f32[4,1,128,128]{3,2,1,0:T(8,128)S(1)} %get-tuple-element.41), channel_id=1, source_target_pairs={{0,4},{4,8},{8,12},{1,5},{5,9},{9,13},{2,6},{6,10},{10,14},{3,7},{... | collective-permute-start | bytes 786440 | tf_op jit(solution)/shard_map/ppermute | solution.py:31
  193.1 6.2 %collective-permute-start.32 = (f32[4,1,128,128]{3,2,1,0:T(8,128)S(1)}, f32[4,1,128,128]{3,2,1,0:T(8,128)S(1)}, u32[]{:S(2)}, u32[]{:S(2)}) collective-permute-start(f32[4,1,128,128]{3,2,1,0:T(8,128)S(1)} %get-tuple-element.39), channel_id=1, source_target_pairs={{0,4},{4,8},{8,12},{1,5},{5,9},{9,13},{2,6},{6,10},{10,14},{3,7},{... | collective-permute-start | bytes 786440 | tf_op jit(solution)/shard_map/ppermute | solution.py:31
  205.7 6.2 %collective-permute-start.36 = (f32[4,1,128,128]{3,2,1,0:T(8,128)S(1)}, f32[4,1,128,128]{3,2,1,0:T(8,128)S(1)}, u32[]{:S(2)}, u32[]{:S(2)}) collective-permute-start(f32[4,1,128,128]{3,2,1,0:T(8,128)S(1)} %get-tuple-element.37), channel_id=1, source_target_pairs={{0,4},{4,8},{8,12},{1,5},{5,9},{9,13},{2,6},{6,10},{10,14},{3,7},{... | collective-permute-start | bytes 786440 | tf_op jit(solution)/shard_map/ppermute | solution.py:31
  213.4 3.9 %collective-permute-done.33 = f32[2,128,128]{2,1,0:T(8,128)S(1)} collective-permute-done((f32[2,128,128]{2,1,0:T(8,128)S(1)}, f32[2,128,128]{2,1,0:T(8,128)S(1)}, u32[]{:S(2)}, u32[]{:S(2)}) %collective-permute-start.33) | collective-permute-done | bytes 131104 | tf_op jit(solution)/shard_map/ppermute | solution.py:12
  217.4 2.9 %collective-permute-start.34 = (f32[2,128,128]{2,1,0:T(8,128)S(1)}, f32[2,128,128]{2,1,0:T(8,128)S(1)}, u32[]{:S(2)}, u32[]{:S(2)}) collective-permute-start(f32[2,128,128]{2,1,0:T(8,128)S(1)} %add.1312), channel_id=1, source_target_pairs={{0,2},{1,3},{2,0},{3,1},{4,6},{5,7},{6,4},{7,5},{8,10},{9,11},{10,... | collective-permute-start | bytes 393224 | tf_op jit(solution)/shard_map/ppermute | solution.py:12
  223.0 3.1 %collective-permute-done.34 = f32[2,128,128]{2,1,0:T(8,128)S(1)} collective-permute-done((f32[2,128,128]{2,1,0:T(8,128)S(1)}, f32[2,128,128]{2,1,0:T(8,128)S(1)}, u32[]{:S(2)}, u32[]{:S(2)}) %collective-permute-start.34) | collective-permute-done | bytes 131104 | tf_op jit(solution)/shard_map/ppermute | solution.py:12
  (381 shorter events, 96.7 us)
Async XLA Ops:
  1.4 27.5 %collective-permute-start = (f32[4,1,128,128]{3,2,1,0:T(8,128)}, f32[4,1,128,128]{3,2,1,0:T(8,128)}, u32[]{:S(2)}, u32[]{:S(2)}) collective-permute-start(f32[4,1,128,128]{3,2,1,0:T(8,128)} %broadcast.302), channel_id=1, source_target_pairs={{4,0},{8,4},{12,8},{5,1},{9,5},{13,9},{6,2},{10,6},{14,10},{7,3},{... | collective-permute-start | bytes 786440 | tf_op jit(solution)/shard_map/ppermute | solution.py:33
  2.8 25.1 %collective-permute-start.1 = (f32[4,1,128,128]{3,2,1,0:T(8,128)}, f32[4,1,128,128]{3,2,1,0:T(8,128)}, u32[]{:S(2)}, u32[]{:S(2)}) collective-permute-start(f32[4,1,128,128]{3,2,1,0:T(8,128)} %broadcast.302), channel_id=1, source_target_pairs={{0,4},{4,8},{8,12},{1,5},{5,9},{9,13},{2,6},{6,10},{10,14},{3,7},{... | collective-permute-start | bytes 786440 | tf_op jit(solution)/shard_map/ppermute | solution.py:31
  8.4 13.8 %collective-permute-start.2 = (bf16[8,1,128,128]{3,2,1,0:T(8,128)(2,1)}, bf16[8,1,128,128]{3,2,1,0:T(8,128)(2,1)}, u32[]{:S(2)}, u32[]{:S(2)}) collective-permute-start(bf16[8,1,128,128]{3,2,1,0:T(8,128)(2,1)} %get-tuple-element.84), channel_id=1, source_target_pairs={{0,4},{4,8},{8,12},{1,5},{5,9},{9,13},{2,6},{6,10},{10,14},{3,7},{... | collective-permute-start | bytes 786440 | tf_op jit(solution)/shard_map/ppermute | solution.py:31
  12.9 10.4 %collective-permute-start.3 = (bf16[8,1,128,128]{3,2,1,0:T(8,128)(2,1)}, bf16[8,1,128,128]{3,2,1,0:T(8,128)(2,1)}, u32[]{:S(2)}, u32[]{:S(2)}) collective-permute-start(bf16[8,1,128,128]{3,2,1,0:T(8,128)(2,1)} %get-tuple-element.83), channel_id=1, source_target_pairs={{4,0},{8,4},{12,8},{5,1},{9,5},{13,9},{6,2},{10,6},{14,10},{7,3},{... | collective-permute-start | bytes 786440 | tf_op jit(solution)/shard_map/ppermute | solution.py:33
  41.4 8.0 %collective-permute-start.6 = (f32[4,1,128,128]{3,2,1,0:T(8,128)S(1)}, f32[4,1,128,128]{3,2,1,0:T(8,128)S(1)}, u32[]{:S(2)}, u32[]{:S(2)}) collective-permute-start(f32[4,1,128,128]{3,2,1,0:T(8,128)S(1)} %get-tuple-element.80), channel_id=1, source_target_pairs={{4,0},{8,4},{12,8},{5,1},{9,5},{13,9},{6,2},{10,6},{14,10},{7,3},{... | collective-permute-start | bytes 786440 | tf_op jit(solution)/shard_map/ppermute | solution.py:33
  42.8 7.6 %collective-permute-start.7 = (f32[4,1,128,128]{3,2,1,0:T(8,128)S(1)}, f32[4,1,128,128]{3,2,1,0:T(8,128)S(1)}, u32[]{:S(2)}, u32[]{:S(2)}) collective-permute-start(f32[4,1,128,128]{3,2,1,0:T(8,128)S(1)} %get-tuple-element.79), channel_id=1, source_target_pairs={{0,4},{4,8},{8,12},{1,5},{5,9},{9,13},{2,6},{6,10},{10,14},{3,7},{... | collective-permute-start | bytes 786440 | tf_op jit(solution)/shard_map/ppermute | solution.py:31
  52.4 8.1 %collective-permute-start.9 = (f32[4,1,128,128]{3,2,1,0:T(8,128)S(1)}, f32[4,1,128,128]{3,2,1,0:T(8,128)S(1)}, u32[]{:S(2)}, u32[]{:S(2)}) collective-permute-start(f32[4,1,128,128]{3,2,1,0:T(8,128)S(1)} %get-tuple-element.77), channel_id=1, source_target_pairs={{0,4},{4,8},{8,12},{1,5},{5,9},{9,13},{2,6},{6,10},{10,14},{3,7},{... | collective-permute-start | bytes 786440 | tf_op jit(solution)/shard_map/ppermute | solution.py:31
  59.0 5.4 %collective-permute-start.8 = (f32[4,1,128,128]{3,2,1,0:T(8,128)S(1)}, f32[4,1,128,128]{3,2,1,0:T(8,128)S(1)}, u32[]{:S(2)}, u32[]{:S(2)}) collective-permute-start(f32[4,1,128,128]{3,2,1,0:T(8,128)S(1)} %get-tuple-element.78), channel_id=1, source_target_pairs={{4,0},{8,4},{12,8},{5,1},{9,5},{13,9},{6,2},{10,6},{14,10},{7,3},{... | collective-permute-start | bytes 786440 | tf_op jit(solution)/shard_map/ppermute | solution.py:33
  66.5 8.4 %collective-permute-start.11 = (f32[4,1,128,128]{3,2,1,0:T(8,128)S(1)}, f32[4,1,128,128]{3,2,1,0:T(8,128)S(1)}, u32[]{:S(2)}, u32[]{:S(2)}) collective-permute-start(f32[4,1,128,128]{3,2,1,0:T(8,128)S(1)} %get-tuple-element.75), channel_id=1, source_target_pairs={{0,4},{4,8},{8,12},{1,5},{5,9},{9,13},{2,6},{6,10},{10,14},{3,7},{... | collective-permute-start | bytes 786440 | tf_op jit(solution)/shard_map/ppermute | solution.py:31
  78.9 8.0 %collective-permute-start.13 = (f32[4,1,128,128]{3,2,1,0:T(8,128)S(1)}, f32[4,1,128,128]{3,2,1,0:T(8,128)S(1)}, u32[]{:S(2)}, u32[]{:S(2)}) collective-permute-start(f32[4,1,128,128]{3,2,1,0:T(8,128)S(1)} %get-tuple-element.73), channel_id=1, source_target_pairs={{0,4},{4,8},{8,12},{1,5},{5,9},{9,13},{2,6},{6,10},{10,14},{3,7},{... | collective-permute-start | bytes 786440 | tf_op jit(solution)/shard_map/ppermute | solution.py:31
  90.8 7.7 %collective-permute-start.15 = (f32[4,1,128,128]{3,2,1,0:T(8,128)S(1)}, f32[4,1,128,128]{3,2,1,0:T(8,128)S(1)}, u32[]{:S(2)}, u32[]{:S(2)}) collective-permute-start(f32[4,1,128,128]{3,2,1,0:T(8,128)S(1)} %get-tuple-element.71), channel_id=1, source_target_pairs={{0,4},{4,8},{8,12},{1,5},{5,9},{9,13},{2,6},{6,10},{10,14},{3,7},{... | collective-permute-start | bytes 786440 | tf_op jit(solution)/shard_map/ppermute | solution.py:31
  102.5 7.9 %collective-permute-start.17 = (f32[4,1,128,128]{3,2,1,0:T(8,128)S(1)}, f32[4,1,128,128]{3,2,1,0:T(8,128)S(1)}, u32[]{:S(2)}, u32[]{:S(2)}) collective-permute-start(f32[4,1,128,128]{3,2,1,0:T(8,128)S(1)} %get-tuple-element.69), channel_id=1, source_target_pairs={{0,4},{4,8},{8,12},{1,5},{5,9},{9,13},{2,6},{6,10},{10,14},{3,7},{... | collective-permute-start | bytes 786440 | tf_op jit(solution)/shard_map/ppermute | solution.py:31
  114.4 12.7 %collective-permute-start.18 = (f32[4,2,128,128]{3,2,1,0:T(8,128)S(1)}, f32[4,2,128,128]{3,2,1,0:T(8,128)S(1)}, u32[]{:S(2)}, u32[]{:S(2)}) collective-permute-start(f32[4,2,128,128]{3,2,1,0:T(8,128)S(1)} %pad_maximum_fusion.2), channel_id=1, source_target_pairs={{0,3},{1,0},{2,1},{3,2},{4,7},{5,4},{6,5},{7,6},{8,11},{9,8},{10,9... | collective-permute-start | bytes 1572872 | tf_op jit(solution)/shard_map/ppermute | solution.py:43
  127.1 6.7 %collective-permute-start.20 = (f32[4,1,128,128]{3,2,1,0:T(8,128)S(1)}, f32[4,1,128,128]{3,2,1,0:T(8,128)S(1)}, u32[]{:S(2)}, u32[]{:S(2)}) collective-permute-start(f32[4,1,128,128]{3,2,1,0:T(8,128)S(1)} %get-tuple-element.51), channel_id=1, source_target_pairs={{0,4},{4,8},{8,12},{1,5},{5,9},{9,13},{2,6},{6,10},{10,14},{3,7},{... | collective-permute-start | bytes 786440 | tf_op jit(solution)/shard_map/ppermute | solution.py:31
  137.4 7.5 %collective-permute-start.22 = (f32[4,1,128,128]{3,2,1,0:T(8,128)S(1)}, f32[4,1,128,128]{3,2,1,0:T(8,128)S(1)}, u32[]{:S(2)}, u32[]{:S(2)}) collective-permute-start(f32[4,1,128,128]{3,2,1,0:T(8,128)S(1)} %get-tuple-element.49), channel_id=1, source_target_pairs={{0,4},{4,8},{8,12},{1,5},{5,9},{9,13},{2,6},{6,10},{10,14},{3,7},{... | collective-permute-start | bytes 786440 | tf_op jit(solution)/shard_map/ppermute | solution.py:31
  148.6 7.5 %collective-permute-start.24 = (f32[4,1,128,128]{3,2,1,0:T(8,128)S(1)}, f32[4,1,128,128]{3,2,1,0:T(8,128)S(1)}, u32[]{:S(2)}, u32[]{:S(2)}) collective-permute-start(f32[4,1,128,128]{3,2,1,0:T(8,128)S(1)} %get-tuple-element.47), channel_id=1, source_target_pairs={{0,4},{4,8},{8,12},{1,5},{5,9},{9,13},{2,6},{6,10},{10,14},{3,7},{... | collective-permute-start | bytes 786440 | tf_op jit(solution)/shard_map/ppermute | solution.py:31
  159.7 7.7 %collective-permute-start.26 = (f32[4,1,128,128]{3,2,1,0:T(8,128)S(1)}, f32[4,1,128,128]{3,2,1,0:T(8,128)S(1)}, u32[]{:S(2)}, u32[]{:S(2)}) collective-permute-start(f32[4,1,128,128]{3,2,1,0:T(8,128)S(1)} %get-tuple-element.45), channel_id=1, source_target_pairs={{0,4},{4,8},{8,12},{1,5},{5,9},{9,13},{2,6},{6,10},{10,14},{3,7},{... | collective-permute-start | bytes 786440 | tf_op jit(solution)/shard_map/ppermute | solution.py:31
  170.9 7.5 %collective-permute-start.28 = (f32[4,1,128,128]{3,2,1,0:T(8,128)S(1)}, f32[4,1,128,128]{3,2,1,0:T(8,128)S(1)}, u32[]{:S(2)}, u32[]{:S(2)}) collective-permute-start(f32[4,1,128,128]{3,2,1,0:T(8,128)S(1)} %get-tuple-element.43), channel_id=1, source_target_pairs={{0,4},{4,8},{8,12},{1,5},{5,9},{9,13},{2,6},{6,10},{10,14},{3,7},{... | collective-permute-start | bytes 786440 | tf_op jit(solution)/shard_map/ppermute | solution.py:31
  182.0 7.5 %collective-permute-start.30 = (f32[4,1,128,128]{3,2,1,0:T(8,128)S(1)}, f32[4,1,128,128]{3,2,1,0:T(8,128)S(1)}, u32[]{:S(2)}, u32[]{:S(2)}) collective-permute-start(f32[4,1,128,128]{3,2,1,0:T(8,128)S(1)} %get-tuple-element.41), channel_id=1, source_target_pairs={{0,4},{4,8},{8,12},{1,5},{5,9},{9,13},{2,6},{6,10},{10,14},{3,7},{... | collective-permute-start | bytes 786440 | tf_op jit(solution)/shard_map/ppermute | solution.py:31
  193.1 7.5 %collective-permute-start.32 = (f32[4,1,128,128]{3,2,1,0:T(8,128)S(1)}, f32[4,1,128,128]{3,2,1,0:T(8,128)S(1)}, u32[]{:S(2)}, u32[]{:S(2)}) collective-permute-start(f32[4,1,128,128]{3,2,1,0:T(8,128)S(1)} %get-tuple-element.39), channel_id=1, source_target_pairs={{0,4},{4,8},{8,12},{1,5},{5,9},{9,13},{2,6},{6,10},{10,14},{3,7},{... | collective-permute-start | bytes 786440 | tf_op jit(solution)/shard_map/ppermute | solution.py:31
  205.7 14.6 %collective-permute-start.36 = (f32[4,1,128,128]{3,2,1,0:T(8,128)S(1)}, f32[4,1,128,128]{3,2,1,0:T(8,128)S(1)}, u32[]{:S(2)}, u32[]{:S(2)}) collective-permute-start(f32[4,1,128,128]{3,2,1,0:T(8,128)S(1)} %get-tuple-element.37), channel_id=1, source_target_pairs={{0,4},{4,8},{8,12},{1,5},{5,9},{9,13},{2,6},{6,10},{10,14},{3,7},{... | collective-permute-start | bytes 786440 | tf_op jit(solution)/shard_map/ppermute | solution.py:31
  211.9 5.5 %collective-permute-start.33 = (f32[2,128,128]{2,1,0:T(8,128)S(1)}, f32[2,128,128]{2,1,0:T(8,128)S(1)}, u32[]{:S(2)}, u32[]{:S(2)}) collective-permute-start(f32[2,128,128]{2,1,0:T(8,128)S(1)} %get-tuple-element.10), channel_id=1, source_target_pairs={{0,1},{1,0},{2,3},{3,2},{4,5},{5,4},{6,7},{7,6},{8,9},{9,8},{10,11... | collective-permute-start | bytes 393224 | tf_op jit(solution)/shard_map/ppermute | solution.py:12
  212.1 8.2 %collective-permute-start.35 = (f32[4,1,128,128]{3,2,1,0:T(8,128)S(1)}, f32[4,1,128,128]{3,2,1,0:T(8,128)S(1)}, u32[]{:S(2)}, u32[]{:S(2)}) collective-permute-start(f32[4,1,128,128]{3,2,1,0:T(8,128)S(1)} %get-tuple-element.38), channel_id=1, source_target_pairs={{4,0},{8,4},{12,8},{5,1},{9,5},{13,9},{6,2},{10,6},{14,10},{7,3},{... | collective-permute-start | bytes 786440 | tf_op jit(solution)/shard_map/ppermute | solution.py:33
  217.4 8.8 %collective-permute-start.34 = (f32[2,128,128]{2,1,0:T(8,128)S(1)}, f32[2,128,128]{2,1,0:T(8,128)S(1)}, u32[]{:S(2)}, u32[]{:S(2)}) collective-permute-start(f32[2,128,128]{2,1,0:T(8,128)S(1)} %add.1312), channel_id=1, source_target_pairs={{0,2},{1,3},{2,0},{3,1},{4,6},{5,7},{6,4},{7,5},{8,10},{9,11},{10,... | collective-permute-start | bytes 393224 | tf_op jit(solution)/shard_map/ppermute | solution.py:12
  (72 other events, 179.0 us)
